TPU v7x, 512 devices: a whole 4x4x16 slice. The times are simulated.
512 devices in a mesh: seq: 128 (over y, z, core), head: 4 (over x).
Axes of the slice: x: 4, y: 4, z: 16, core: 2. Of those that a mesh axis runs over, the one named last changes fastest.
Arguments:
- tokens: bfloat16 [64, 4, 1024], P('head'), may hold values from -6 to 6
- cache_keys: bfloat16 [64, 4096, 512], P(None, 'seq', 'head'), may hold values from -70 to 70
- cache_values: bfloat16 [64, 4096, 512], P(None, 'seq', 'head'), may hold values from -6 to 6
- held_states: bfloat16 [64, 512, 1024], P(None, 'seq'), may hold values from -6 to 6
- recompute_pos: int32 [64, 512], P(None, 'seq'), may hold values from 0 to 4095, as said below
- cache_len: int32 [64], replicated, may hold values from 1 to 4096
- new_prompt: int32 [64], replicated, may hold values 0 or 1
- w_qkv: bfloat16 [3, 1024, 512], P(None, None, 'head'), may hold values from -0.1875 to 0.1875
- qkv_bias: float32 [3, 512], P(None, 'head'), may hold values from -3 to 3
- w_out: bfloat16 [512, 1024], P('head'), may hold values from -1.5 to 1.5
- out_bias: float32 [1024], replicated, may hold values from -3 to 3
- attn_gain: float32 [1024], replicated, may hold values from 0.1 to 1.9
- attn_shift: float32 [1024], replicated, may hold values from -3 to 3
- w_up: bfloat16 [1024, 2048], P(None, 'head'), may hold values from -0.1875 to 0.1875
- up_bias: float32 [2048], P('head'), may hold values from -3 to 3
- w_down: bfloat16 [2048, 1024], P('head'), may hold values from -0.125 to 0.125
- down_bias: float32 [1024], replicated, may hold values from -3 to 3
- ffn_gain: float32 [1024], replicated, may hold values from 0.1 to 1.9
- ffn_shift: float32 [1024], replicated, may hold values from -3 to 3
Outputs:
- layer_out: bfloat16 [64, 4, 1024], P('head')
Inputs may be any that keep to these rules, and one draw needn't show every extreme that they name: `recompute_pos`: columns s * 4 to (s + 1) * 4 - 1 of a row hold distinct positions from s * 32 to (s + 1) * 32 - 1.
All inputs are finite; a program needn't handle non-finite values.
Results may differ from a plain program's by a relative error of at most 0.011.
Values may be sent and summed in bfloat16 or wider, within the bound.
No kernel may reach another device: no remote copies, remote signals or barrier semaphores. Data moves between devices by JAX's collectives and lax.ppermute only.
A program may use at most 192 MiB of HBM per device.

v0:
```python
import jax
import jax.numpy as jnp
from jax import lax
from jax.sharding import PartitionSpec as P

HDIM = 64
NEG = -1e30
EPS = 1e-05


def layer_norm(values, norm_gain, norm_bias):
    center = jnp.mean(values, axis=-1, keepdims=True)
    spread = values - center
    second = jnp.mean(spread * spread, axis=-1, keepdims=True)
    return spread * lax.rsqrt(second + EPS) * norm_gain + norm_bias


def merge_pair(first_part, second_part):
    first_max, first_sum, first_out = first_part
    second_max, second_sum, second_out = second_part
    joint_max = jnp.maximum(first_max, second_max)
    first_scale = jnp.exp(first_max - joint_max)
    second_scale = jnp.exp(second_max - joint_max)
    return (
        joint_max,
        first_sum * first_scale + second_sum * second_scale,
        first_out * first_scale[..., None] + second_out * second_scale[..., None],
    )


def partial_attention(queries, keys_here, values_here, visible):
    scores = jnp.einsum(
        "rthe,rphe->rthp", queries, keys_here, preferred_element_type=jnp.float32
    ) * HDIM ** (-0.5)
    highest = jnp.max(jnp.where(visible, scores, NEG), axis=-1)
    weights = jnp.exp(jnp.where(visible, scores - highest[..., None], NEG)).astype(jnp.bfloat16)
    totals = jnp.sum(weights.astype(jnp.float32), axis=-1)
    blended = jnp.einsum(
        "rthp,rphe->rthe", weights, values_here, preferred_element_type=jnp.float32
    )
    return (highest, totals, blended)


def seq_merge(block_max, block_sum, block_out):
    n_seq = lax.axis_size("seq")
    head_shape = block_out.shape
    lanes = head_shape[-2] * head_shape[-1]
    rows = block_out.size // lanes
    stat_rows = block_max.size // lanes
    out2 = block_out.reshape(rows, lanes)
    top = block_max.reshape(stat_rows, lanes)
    total = block_sum.reshape(stat_rows, lanes)
    width = head_shape[-1]
    step = 1
    while step < n_seq:
        pairs = [(i, i ^ step) for i in range(n_seq)]
        packed = jnp.concatenate([out2, top, total], axis=0)
        other = lax.ppermute(packed, "seq", pairs)
        o_out = other[:rows]
        o_top = other[rows : rows + stat_rows]
        o_total = other[rows + stat_rows :]
        joint = jnp.maximum(top, o_top)
        mine = jnp.exp(top - joint)
        theirs = jnp.exp(o_top - joint)
        total = total * mine + o_total * theirs
        mine_rows = jnp.repeat(mine.reshape(rows, lanes // width), width, axis=1)
        theirs_rows = jnp.repeat(theirs.reshape(rows, lanes // width), width, axis=1)
        out2 = out2 * mine_rows + o_out * theirs_rows
        top = joint
        step *= 2
    return (top.reshape(block_max.shape), total.reshape(block_sum.shape), out2.reshape(head_shape))


def on_device(
    tokens,
    cache_keys,
    cache_values,
    held_states,
    recompute_pos,
    cache_len,
    new_prompt,
    w_qkv,
    qkv_bias,
    w_out,
    out_bias,
    attn_gain,
    attn_shift,
    w_up,
    up_bias,
    w_down,
    down_bias,
    ffn_gain,
    ffn_shift,
):
    local_width = w_qkv.shape[2]
    local_heads = local_width // HDIM
    requests = cache_keys.shape[0]
    block_len = cache_keys.shape[1]
    own_rows = tokens.shape[0]
    steps_count = tokens.shape[1]
    block_rows = lax.all_gather(tokens, "head", axis=0, tiled=True)
    triple = (
        jnp.einsum("rtd,kdc->rtkc", block_rows, w_qkv, preferred_element_type=jnp.float32)
        + qkv_bias
    )
    triple = triple.astype(jnp.bfloat16).reshape(
        block_rows.shape[0], block_rows.shape[1], 3 * local_width
    )
    gathered = jnp.concatenate([triple, block_rows], axis=2)
    head_shape = (requests, steps_count, local_heads, HDIM)
    queries = gathered[:, :, :local_width].reshape(head_shape)
    new_keys = gathered[:, :, local_width : 2 * local_width].reshape(head_shape)
    new_values = gathered[:, :, 2 * local_width : 3 * local_width].reshape(head_shape)
    fresh_keys = (
        jnp.einsum("rjd,dc->rjc", held_states, w_qkv[1], preferred_element_type=jnp.float32)
        + qkv_bias[1]
    ).astype(jnp.bfloat16)
    offset_pos = lax.axis_index("seq") * block_len
    positions = jnp.arange(block_len, dtype=jnp.int32)
    matches = (recompute_pos - offset_pos)[:, :, None] == positions[None, None, :]
    placed = jnp.einsum(
        "rjp,rjc->rpc", matches.astype(jnp.bfloat16), fresh_keys, preferred_element_type=jnp.float32
    ).astype(jnp.bfloat16)
    replaced = jnp.any(matches, axis=1)
    keys_here = jnp.where(replaced[:, :, None], placed, cache_keys).reshape(
        requests, block_len, local_heads, HDIM
    )
    values_here = cache_values.reshape(requests, block_len, local_heads, HDIM)
    visible = ((offset_pos + positions)[None, :] < cache_len[:, None]) & (new_prompt[:, None] == 0)
    block_max, block_sum, block_out = partial_attention(
        queries, keys_here, values_here, visible[:, None, None, :]
    )
    cache_max, cache_sum, cache_out = seq_merge(block_max, block_sum, block_out)
    order_t = jnp.arange(steps_count, dtype=jnp.int32)
    causal = (order_t[:, None] >= order_t[None, :])[None, :, None, :]
    new_max, new_sum, new_out = partial_attention(queries, new_keys, new_values, causal)
    joint_max, joint_sum, joint_out = merge_pair(
        (cache_max, cache_sum, cache_out), (new_max, new_sum, new_out)
    )
    attended = (
        (joint_out / joint_sum[..., None])
        .astype(jnp.bfloat16)
        .reshape(requests, steps_count, local_width)
    )
    head_terms = jnp.einsum("rtc,cd->rtd", attended, w_out, preferred_element_type=jnp.float32)
    summed = lax.psum(head_terms, "head")
    inputs_all = gathered[:, :, 3 * local_width :]
    normed_all = layer_norm(
        inputs_all.astype(jnp.float32) + summed + out_bias, attn_gain, attn_shift
    ).astype(jnp.bfloat16)
    hidden_all = jax.nn.gelu(
        jnp.einsum("rtd,df->rtf", normed_all, w_up, preferred_element_type=jnp.float32) + up_bias,
        approximate=False,
    ).astype(jnp.bfloat16)
    normed = lax.dynamic_slice_in_dim(normed_all, lax.axis_index("head") * own_rows, own_rows, 0)
    reduced = lax.psum_scatter(
        jnp.einsum("rtf,fd->rtd", hidden_all, w_down, preferred_element_type=jnp.float32),
        "head",
        scatter_dimension=0,
        tiled=True,
    )
    return layer_norm(normed.astype(jnp.float32) + reduced + down_bias, ffn_gain, ffn_shift).astype(
        jnp.bfloat16
    )


def solution(mesh):
    placed = (
        P("head", None, None),
        P(None, "seq", "head"),
        P(None, "seq", "head"),
        P(None, "seq", None),
        P(None, "seq"),
        P(),
        P(),
        P(None, None, "head"),
        P(None, "head"),
        P("head", None),
        P(),
        P(),
        P(),
        P(None, "head"),
        P("head"),
        P("head", None),
        P(),
        P(),
        P(),
    )
    return jax.shard_map(
        on_device, mesh=mesh, in_specs=placed, out_specs=P("head", None, None), check_vma=False
    )
```

profile of v0, /device:TPU:8, one launch (start us, length us, event | category | flops | bytes accessed | tf_op | source)
XLA Modules:
  0.0 232.6 jit_solution(7463980318247415298)
XLA Ops:
  9.0 1.0 copy.122
  10.0 13.1 %all_gather.3 = bf16[64,4,1024]{2,0,1:T(8,128)(2,1)S(1)} all-gather(bf16[16,4,1024]{2,0,1:T(8,128)(2,1)S(1)} %copy.122), channel_id=1, replica_groups=mesh['seq'=128,'head'=4] {'head'}, dimensions={0}, use_global_device_ids=true | all-gather | bytes 655360 | tf_op jit(solution)/shard_map/all_gather | solution.py:101
  27.7 1.7 select_reduce_fusion
  32.4 1.9 collective-permute-start
  34.3 1.3 collective-permute-done
  36.4 3.8 %collective-permute-start.1 = (f32[264,128]{1,0:T(8,128)S(1)}, f32[264,128]{1,0:T(8,128)S(1)}, u32[]{:S(2)}, u32[]{:S(2)}) collective-permute-start(f32[264,128]{1,0:T(8,128)S(1)} %pad_maximum_fusion.1), channel_id=1, source_target_pairs={{0,8},{4,12},{8,0},{12,4},{16,24},{20,28},{24,16},{28,20},{32,40},... | collective-permute-start | bytes 405512 | tf_op jit(solution)/shard_map/ppermute | solution.py:58
  40.3 3.9 %collective-permute-done.1 = f32[264,128]{1,0:T(8,128)S(1)} collective-permute-done((f32[264,128]{1,0:T(8,128)S(1)}, f32[264,128]{1,0:T(8,128)S(1)}, u32[]{:S(2)}, u32[]{:S(2)}) %collective-permute-start.1) | collective-permute-done | bytes 135200 | tf_op jit(solution)/shard_map/ppermute | solution.py:58
  44.9 5.2 %collective-permute-start.2 = (f32[264,128]{1,0:T(8,128)S(1)}, f32[264,128]{1,0:T(8,128)S(1)}, u32[]{:S(2)}, u32[]{:S(2)}) collective-permute-start(f32[264,128]{1,0:T(8,128)S(1)} %pad_maximum_fusion.2), channel_id=1, source_target_pairs={{0,16},{4,20},{8,24},{12,28},{16,0},{20,4},{24,8},{28,12},{32,48},... | collective-permute-start | bytes 405512 | tf_op jit(solution)/shard_map/ppermute | solution.py:58
  50.1 6.1 %collective-permute-done.2 = f32[264,128]{1,0:T(8,128)S(1)} collective-permute-done((f32[264,128]{1,0:T(8,128)S(1)}, f32[264,128]{1,0:T(8,128)S(1)}, u32[]{:S(2)}, u32[]{:S(2)}) %collective-permute-start.2) | collective-permute-done | bytes 135200 | tf_op jit(solution)/shard_map/ppermute | solution.py:58
  57.0 9.1 %collective-permute-start.3 = (f32[264,128]{1,0:T(8,128)S(1)}, f32[264,128]{1,0:T(8,128)S(1)}, u32[]{:S(2)}, u32[]{:S(2)}) collective-permute-start(f32[264,128]{1,0:T(8,128)S(1)} %pad_maximum_fusion.3), channel_id=1, source_target_pairs={{0,32},{4,36},{8,40},{12,44},{16,48},{20,52},{24,56},{28,60},{32,0... | collective-permute-start | bytes 405512 | tf_op jit(solution)/shard_map/ppermute | solution.py:58
  66.2 10.2 %collective-permute-done.3 = f32[264,128]{1,0:T(8,128)S(1)} collective-permute-done((f32[264,128]{1,0:T(8,128)S(1)}, f32[264,128]{1,0:T(8,128)S(1)}, u32[]{:S(2)}, u32[]{:S(2)}) %collective-permute-start.3) | collective-permute-done | bytes 135200 | tf_op jit(solution)/shard_map/ppermute | solution.py:58
  77.1 13.6 %collective-permute-start.4 = (f32[264,128]{1,0:T(8,128)S(1)}, f32[264,128]{1,0:T(8,128)S(1)}, u32[]{:S(2)}, u32[]{:S(2)}) collective-permute-start(f32[264,128]{1,0:T(8,128)S(1)} %pad_maximum_fusion.4), channel_id=1, source_target_pairs={{0,64},{4,68},{8,72},{12,76},{16,80},{20,84},{24,88},{28,92},{32,9... | collective-permute-start | bytes 405512 | tf_op jit(solution)/shard_map/ppermute | solution.py:58
  91.0 12.1 %collective-permute-done.4 = f32[264,128]{1,0:T(8,128)S(1)} collective-permute-done((f32[264,128]{1,0:T(8,128)S(1)}, f32[264,128]{1,0:T(8,128)S(1)}, u32[]{:S(2)}, u32[]{:S(2)}) %collective-permute-start.4) | collective-permute-done | bytes 135200 | tf_op jit(solution)/shard_map/ppermute | solution.py:58
  103.9 3.5 %collective-permute-start.5 = (f32[264,128]{1,0:T(8,128)S(1)}, f32[264,128]{1,0:T(8,128)S(1)}, u32[]{:S(2)}, u32[]{:S(2)}) collective-permute-start(f32[264,128]{1,0:T(8,128)S(1)} %pad_maximum_fusion.5), channel_id=1, source_target_pairs={{0,128},{4,132},{8,136},{12,140},{16,144},{20,148},{24,152},{28,15... | collective-permute-start | bytes 405512 | tf_op jit(solution)/shard_map/ppermute | solution.py:58
  107.8 3.3 %collective-permute-done.5 = f32[264,128]{1,0:T(8,128)S(1)} collective-permute-done((f32[264,128]{1,0:T(8,128)S(1)}, f32[264,128]{1,0:T(8,128)S(1)}, u32[]{:S(2)}, u32[]{:S(2)}) %collective-permute-start.5) | collective-permute-done | bytes 135200 | tf_op jit(solution)/shard_map/ppermute | solution.py:58
  111.9 3.9 %collective-permute-start.6 = (f32[264,128]{1,0:T(8,128)S(1)}, f32[264,128]{1,0:T(8,128)S(1)}, u32[]{:S(2)}, u32[]{:S(2)}) collective-permute-start(f32[264,128]{1,0:T(8,128)S(1)} %pad_maximum_fusion.6), channel_id=1, source_target_pairs={{0,256},{4,260},{8,264},{12,268},{16,272},{20,276},{24,280},{28,28... | collective-permute-start | bytes 405512 | tf_op jit(solution)/shard_map/ppermute | solution.py:58
  116.1 4.2 %collective-permute-done.6 = f32[264,128]{1,0:T(8,128)S(1)} collective-permute-done((f32[264,128]{1,0:T(8,128)S(1)}, f32[264,128]{1,0:T(8,128)S(1)}, u32[]{:S(2)}, u32[]{:S(2)}) %collective-permute-start.6) | collective-permute-done | bytes 135200 | tf_op jit(solution)/shard_map/ppermute | solution.py:58
  123.7 1.3 fusion.29
  125.3 58.1 %all-reduce.2.cloned.1.call-done = f32[64,4,1024]{2,0,1:T(8,128)} async-done(((f32[64,4,1024]{2,0,1:T(8,128)}), f32[64,4,1024]{2,0,1:T(8,128)}) %all-reduce.2.cloned.1.call-update) | async-done | bytes 1048592 | tf_op jit(solution)/shard_map/psum | solution.py:146
  183.4 1.5 fusion.26
  186.3 0.9 copy-done.16
  187.8 2.5 %fusion.9 = f32[64,4,1024]{2,0,1:T(8,128)} fusion(bf16[512,1024]{1,0:T(8,128)(2,1)S(1)} %copy-done, f32[64,4,512]{2,0,1:T(8,128)S(1)} %get-tuple-element.45, u8[64,512]{1,0:T(8,128)(4,1)S(1)} %get-tuple-element.6, u8[64,512]{1,0:T(8,128)(4,1)S(1)} %get-tuple-element.5), kind=kOutput, calls=%fused_computation.16 | convolution fusion | flops 277610496 | bytes 2686976 | tf_op jit(solution)/shard_map/rtf,fd->rtd/dot_general | solution.py:157
  190.3 32.6 %reduce-scatter.2.cloned.1.call-done = f32[16,4,1024]{2,0,1:T(8,128)} async-done(((f32[64,4,1024]{2,0,1:T(8,128)}), f32[16,4,1024]{2,0,1:T(8,128)}) %reduce-scatter.2.cloned.1.call-update) | async-done | bytes 262160 | tf_op jit(solution)/shard_map/reduce_scatter | solution.py:156
  222.9 1.1 fusion.82
  (173 shorter events, 22.4 us)
Async XLA Ops:
  6.5 181.2 %copy-start = (bf16[512,1024]{1,0:T(8,128)(2,1)S(1)}, bf16[512,1024]{1,0:T(8,128)(2,1)}, u32[]{:S(2)}) copy-start(bf16[512,1024]{1,0:T(8,128)(2,1)} %param.34) | copy-start | bytes 3145732
  6.5 16.6 %copy-start.3 = (bf16[3,1024,128]{2,1,0:T(8,128)(2,1)S(1)}, bf16[3,1024,128]{2,1,0:T(8,128)(2,1)}, u32[]{:S(2)}) copy-start(bf16[3,1024,128]{2,1,0:T(8,128)(2,1)} %param.26) | copy-start | bytes 2359300
  6.5 176.9 %all-reduce.2.cloned.1.call-start = ((), (), s32[]{:S(2)}) async-start(), calls=%async_computation.1 | async-start | bytes 2097152 | tf_op jit(solution)/shard_map/psum | solution.py:146
  9.9 13.2 %copy-start.14 = (f32[3,128]{1,0:T(4,128)S(1)}, f32[3,128]{1,0:T(4,128)}, u32[]{:S(2)}) copy-start(f32[3,128]{1,0:T(4,128)} %param.27) | copy-start | bytes 4612
  23.5 1.5 copy-start.17
  25.0 1.0 copy-start.18
  29.4 1.8 copy-start.4
  32.4 3.2 %collective-permute-start = (f32[264,128]{1,0:T(8,128)S(1)}, f32[264,128]{1,0:T(8,128)S(1)}, u32[]{:S(2)}, u32[]{:S(2)}) collective-permute-start(f32[264,128]{1,0:T(8,128)S(1)} %pad_maximum_fusion), channel_id=1, source_target_pairs={{0,4},{4,0},{8,12},{12,8},{16,20},{20,16},{24,28},{28,24},{32,36},... | collective-permute-start | bytes 405512 | tf_op jit(solution)/shard_map/ppermute | solution.py:58
  36.4 7.7 %collective-permute-start.1 = (f32[264,128]{1,0:T(8,128)S(1)}, f32[264,128]{1,0:T(8,128)S(1)}, u32[]{:S(2)}, u32[]{:S(2)}) collective-permute-start(f32[264,128]{1,0:T(8,128)S(1)} %pad_maximum_fusion.1), channel_id=1, source_target_pairs={{0,8},{4,12},{8,0},{12,4},{16,24},{20,28},{24,16},{28,20},{32,40},... | collective-permute-start | bytes 405512 | tf_op jit(solution)/shard_map/ppermute | solution.py:58
  44.9 11.3 %collective-permute-start.2 = (f32[264,128]{1,0:T(8,128)S(1)}, f32[264,128]{1,0:T(8,128)S(1)}, u32[]{:S(2)}, u32[]{:S(2)}) collective-permute-start(f32[264,128]{1,0:T(8,128)S(1)} %pad_maximum_fusion.2), channel_id=1, source_target_pairs={{0,16},{4,20},{8,24},{12,28},{16,0},{20,4},{24,8},{28,12},{32,48},... | collective-permute-start | bytes 405512 | tf_op jit(solution)/shard_map/ppermute | solution.py:58
  56.9 9.1 %copy-start.5 = (bf16[64,4,128]{2,0,1:T(8,128)(2,1)S(1)}, bf16[64,4,128]{2,0,1:T(8,128)(2,1)}, u32[]{:S(2)}) copy-start(bf16[64,4,128]{2,0,1:T(8,128)(2,1)} %get-tuple-element.41) | copy-start | bytes 196612
  57.0 19.4 %collective-permute-start.3 = (f32[264,128]{1,0:T(8,128)S(1)}, f32[264,128]{1,0:T(8,128)S(1)}, u32[]{:S(2)}, u32[]{:S(2)}) collective-permute-start(f32[264,128]{1,0:T(8,128)S(1)} %pad_maximum_fusion.3), channel_id=1, source_target_pairs={{0,32},{4,36},{8,40},{12,44},{16,48},{20,52},{24,56},{28,60},{32,0... | collective-permute-start | bytes 405512 | tf_op jit(solution)/shard_map/ppermute | solution.py:58
  77.1 13.6 %copy-start.7 = (bf16[64,4,2,64]{3,2,0,1:T(2,128)(2,1)S(1)}, bf16[64,4,2,64]{3,2,0,1:T(2,128)(2,1)}, u32[]{:S(2)}) copy-start(bf16[64,4,2,64]{3,2,0,1:T(2,128)(2,1)} %reshape.249) | copy-start | bytes 196612
  77.1 26.0 %collective-permute-start.4 = (f32[264,128]{1,0:T(8,128)S(1)}, f32[264,128]{1,0:T(8,128)S(1)}, u32[]{:S(2)}, u32[]{:S(2)}) collective-permute-start(f32[264,128]{1,0:T(8,128)S(1)} %pad_maximum_fusion.4), channel_id=1, source_target_pairs={{0,64},{4,68},{8,72},{12,76},{16,80},{20,84},{24,88},{28,92},{32,9... | collective-permute-start | bytes 405512 | tf_op jit(solution)/shard_map/ppermute | solution.py:58
  103.9 7.2 %collective-permute-start.5 = (f32[264,128]{1,0:T(8,128)S(1)}, f32[264,128]{1,0:T(8,128)S(1)}, u32[]{:S(2)}, u32[]{:S(2)}) collective-permute-start(f32[264,128]{1,0:T(8,128)S(1)} %pad_maximum_fusion.5), channel_id=1, source_target_pairs={{0,128},{4,132},{8,136},{12,140},{16,144},{20,148},{24,152},{28,15... | collective-permute-start | bytes 405512 | tf_op jit(solution)/shard_map/ppermute | solution.py:58
  111.9 8.4 %collective-permute-start.6 = (f32[264,128]{1,0:T(8,128)S(1)}, f32[264,128]{1,0:T(8,128)S(1)}, u32[]{:S(2)}, u32[]{:S(2)}) collective-permute-start(f32[264,128]{1,0:T(8,128)S(1)} %pad_maximum_fusion.6), channel_id=1, source_target_pairs={{0,256},{4,260},{8,264},{12,268},{16,272},{20,276},{24,280},{28,28... | collective-permute-start | bytes 405512 | tf_op jit(solution)/shard_map/ppermute | solution.py:58
  125.1 58.4 %copy-start.8 = (f32[1024]{0:T(1024)S(1)}, f32[1024]{0:T(1024)}, u32[]{:S(2)}) copy-start(f32[1024]{0:T(1024)} %param.29) | copy-start | bytes 12292
  125.1 97.8 %reduce-scatter.2.cloned.1.call-start = ((), (), s32[]{:S(2)}) async-start(), calls=%async_computation.2 | async-start | bytes 1310720 | tf_op jit(solution)/shard_map/reduce_scatter | solution.py:156
  183.4 1.5 copy-start.1
  186.0 1.2 copy-start.16
  186.0 1.2 copy-start.19
  190.3 32.6 %copy-start.9 = (f32[1024]{0:T(1024)S(1)}, f32[1024]{0:T(1024)}, u32[]{:S(2)}) copy-start(f32[1024]{0:T(1024)} %param.35) | copy-start | bytes 12292
  222.9 1.1 copy-start.2
  222.9 1.4 copy-start.13
  (5 other events, 3.7 us)
Sparse Core Ops, SparseCore 0:
  125.2 58.1 all-reduce.1
  190.4 32.4 reduce-scatter.1
where the time goes:
time: 233 us
  waiting for transfers between devices  132 us (57%)
  starting transfers between devices  41.2 us (18%)
  local copies, waits for them, and re-layouts  16.8 us (7%)
  between operations  14.3 us (6%)
  blocking collectives  13.1 us (6%)
  matrix products  8.92 us (4%)
  other arithmetic  6.39 us (3%)
    psum x1, waiting for transfers between devices, on_device(): summed = lax.psum(head_terms, 'head')  58.1 us
    ppermute x7, waiting for transfers between devices, seq_merge(): other = lax.ppermute(packed, 'seq', pairs)  41.2 us
    ppermute x7, starting transfers between devices, seq_merge(): other = lax.ppermute(packed, 'seq', pairs)  41 us
    reduce_scatter x1, waiting for transfers between devices, on_device(): lax.psum_scatter(jnp.einsum('rtf,fd->rtd', hidden_all, w_down, preferred_...  32.6 us
    all_gather x1, blocking collectives, on_device(): block_rows = lax.all_gather(tokens, 'head', axis=0, tiled=True)  13.1 us
    unnamed x41, local copies, waits for them, and re-layouts  4.99 us
  transfers between devices with their start and end apart: 9, of which 9 were waited for; matrix products, arithmetic and copies ran while one was open for 0% of the time, Pallas kernels for 0%

commit v1 on v0

--- a/solution.py
+++ b/solution.py
@@ -2,6 +2,7 @@
 import jax.numpy as jnp
 from jax import lax
 from jax.sharding import PartitionSpec as P
+from jax.lax import axis_index, axis_size, ppermute
 
 HDIM = 64
 NEG = -1e30
@@ -98,7 +99,19 @@
     block_len = cache_keys.shape[1]
     own_rows = tokens.shape[0]
     steps_count = tokens.shape[1]
-    block_rows = lax.all_gather(tokens, "head", axis=0, tiled=True)
+    cores_n = axis_size("head")
+    tray = tuple(((t, (t + 1) % cores_n) for t in range(cores_n)))
+    gallery = tuple(((t, (t - 1) % cores_n) for t in range(cores_n)))
+    item_now, a_next = ([tokens], [tokens])
+    for _ in range(cores_n // 2):
+        moved = ppermute(item_now[-1], "head", perm=tray)
+        item_now.append(moved)
+    for _ in tuple(range((cores_n - 1) // 2)):
+        view_out = ppermute(a_next[-1], "head", gallery)
+        a_next.append(view_out)
+    mid_arr = jnp.concatenate([*item_now[::-1], *a_next[1:]], 0)
+    r_now = axis_index("head")
+    block_rows = jnp.roll(mid_arr, (r_now - cores_n // 2) * tokens.shape[0], 0)
     triple = (
         jnp.einsum("rtd,kdc->rtkc", block_rows, w_qkv, preferred_element_type=jnp.float32)
         + qkv_bias

time: 233 us -> 237 us (1.017)
  blocking collectives: 13.1 us -> 0 us
  starting transfers between devices: 41.2 us -> 50.5 us
  waiting for transfers between devices: 132 us -> 135 us
    all_gather x1 -> x0, blocking collectives: 13.1 us -> none  [on_device(): block_rows = lax.all_gather(tokens, 'head', axis=0, tiled=True)]
    ppermute x0 -> x3, starting transfers between devices: none -> 9.24 us  [the longest x2 5.59 us: on_device(): moved = ppermute(item_now[-1], 'head', perm=tray)]
    ppermute x0 -> x3, waiting for transfers between devices: none -> 5.78 us  [the longest x2 5.78 us: on_device(): moved = ppermute(item_now[-1], 'head', perm=tray)]
    unnamed x41 -> x56, local copies, waits for them, and re-layouts: 4.99 us -> 7.25 us
  transfers between devices with their start and end apart: 9 -> 12, of which waited for: 9 -> 10; matrix products, arithmetic and copies ran while one was open for 0% -> 2% of each run, Pallas kernels for 0% -> 0%
where the time goes in v1:
time: 237 us; the launch traced here: 236 us
  waiting for transfers between devices  135 us (57%)
  starting transfers between devices  50.5 us (21%)
  local copies, waits for them, and re-layouts  18.8 us (8%)
  between operations  14.5 us (6%)
  matrix products  11.1 us (5%)
  other arithmetic  5.87 us (2%)
    psum x1, waiting for transfers between devices, on_device(): summed = lax.psum(head_terms, 'head')  55.8 us
    ppermute x7, waiting for transfers between devices, seq_merge(): other = lax.ppermute(packed, 'seq', pairs)  41.2 us
    ppermute x7, starting transfers between devices, seq_merge(): other = lax.ppermute(packed, 'seq', pairs)  41 us
    reduce_scatter x1, waiting for transfers between devices, on_device(): lax.psum_scatter(jnp.einsum('rtf,fd->rtd', hidden_all, w_down, preferred_...  32.6 us
    unnamed x56, local copies, waits for them, and re-layouts  7.25 us
    ppermute x2, waiting for transfers between devices, on_device(): moved = ppermute(item_now[-1], 'head', perm=tray)  5.78 us
    ppermute x2, starting transfers between devices, on_device(): moved = ppermute(item_now[-1], 'head', perm=tray)  5.59 us
  transfers between devices with their start and end apart: 12, of which 10 were waited for; matrix products, arithmetic and copies ran while one was open for 2% of the time, Pallas kernels for 0%

profile of v1, /device:TPU:8, one launch (start us, length us, event | category | flops | bytes accessed | tf_op | source)
XLA Modules:
  0.0 236.0 jit_solution(14033944574964702933)
XLA Ops:
  7.6 3.4 %collective-permute-start = (bf16[16,4,1024]{2,0,1:T(8,128)(2,1)S(1)}, bf16[16,4,1024]{2,0,1:T(8,128)(2,1)S(1)}, u32[]{:S(2)}, u32[]{:S(2)}) collective-permute-start(bf16[16,4,1024]{2,0,1:T(8,128)(2,1)S(1)} %copy.131), channel_id=1, source_target_pairs={{0,1},{1,2},{2,3},{3,0},{4,5},{5,6},{6,7},{7,4},{8,9},{9,10},{10,1... | collective-permute-start | bytes 393224 | tf_op jit(solution)/shard_map/ppermute | solution.py:107
  11.0 3.7 %collective-permute-start.2 = (bf16[16,4,1024]{2,0,1:T(8,128)(2,1)S(1)}, bf16[16,4,1024]{2,0,1:T(8,128)(2,1)S(1)}, u32[]{:S(2)}, u32[]{:S(2)}) collective-permute-start(bf16[16,4,1024]{2,0,1:T(8,128)(2,1)S(1)} %copy.131), channel_id=1, source_target_pairs={{0,3},{1,0},{2,1},{3,2},{4,7},{5,4},{6,5},{7,6},{8,11},{9,8},{10,9... | collective-permute-start | bytes 393224 | tf_op jit(solution)/shard_map/ppermute | solution.py:110
  16.1 1.5 fusion.8
  20.5 2.2 collective-permute-start.1
  22.8 5.8 %collective-permute-done.1 = bf16[16,4,1024]{2,0,1:T(8,128)(2,1)S(1)} collective-permute-done((bf16[16,4,1024]{2,0,1:T(8,128)(2,1)S(1)}, bf16[16,4,1024]{2,0,1:T(8,128)(2,1)S(1)}, u32[]{:S(2)}, u32[]{:S(2)}) %collective-permute-start.1) | collective-permute-done | bytes 131104 | tf_op jit(solution)/shard_map/ppermute | solution.py:107
  31.9 2.7 %select_reduce_fusion = (f32[64,4,2]{1,2,0:T(2,128)S(1)}, f32[64,4,2,32]{3,1,2,0:T(4,128)}) fusion(pred[64,32]{1,0:T(8,128)(4,1)S(1)} %compare_and_fusion, bf16[64,4,2,64]{3,2,0,1:T(2,128)(2,1)S(1)} %reshape.249, bf16[64,32,2,64]{3,2,1,0:T(2,128)(2,1)} %reshape.247), kind=kOutput, calls=%fused_computation.90 | convolution fusion | flops 2145792 | bytes 659456 | tf_op jit(solution)/shard_map/rthe,rphe->rthp/dot_general | solution.py:33
  35.1 1.4 convert_reduce_fusion
  38.1 1.9 collective-permute-start.3
  42.1 3.8 %collective-permute-start.4 = (f32[264,128]{1,0:T(8,128)S(1)}, f32[264,128]{1,0:T(8,128)S(1)}, u32[]{:S(2)}, u32[]{:S(2)}) collective-permute-start(f32[264,128]{1,0:T(8,128)S(1)} %pad_maximum_fusion.1), channel_id=1, source_target_pairs={{0,8},{4,12},{8,0},{12,4},{16,24},{20,28},{24,16},{28,20},{32,40},... | collective-permute-start | bytes 405512 | tf_op jit(solution)/shard_map/ppermute | solution.py:59
  46.0 3.9 %collective-permute-done.4 = f32[264,128]{1,0:T(8,128)S(1)} collective-permute-done((f32[264,128]{1,0:T(8,128)S(1)}, f32[264,128]{1,0:T(8,128)S(1)}, u32[]{:S(2)}, u32[]{:S(2)}) %collective-permute-start.4) | collective-permute-done | bytes 135200 | tf_op jit(solution)/shard_map/ppermute | solution.py:59
  50.6 5.2 %collective-permute-start.5 = (f32[264,128]{1,0:T(8,128)S(1)}, f32[264,128]{1,0:T(8,128)S(1)}, u32[]{:S(2)}, u32[]{:S(2)}) collective-permute-start(f32[264,128]{1,0:T(8,128)S(1)} %pad_maximum_fusion.2), channel_id=1, source_target_pairs={{0,16},{4,20},{8,24},{12,28},{16,0},{20,4},{24,8},{28,12},{32,48},... | collective-permute-start | bytes 405512 | tf_op jit(solution)/shard_map/ppermute | solution.py:59
  55.8 6.1 %collective-permute-done.5 = f32[264,128]{1,0:T(8,128)S(1)} collective-permute-done((f32[264,128]{1,0:T(8,128)S(1)}, f32[264,128]{1,0:T(8,128)S(1)}, u32[]{:S(2)}, u32[]{:S(2)}) %collective-permute-start.5) | collective-permute-done | bytes 135200 | tf_op jit(solution)/shard_map/ppermute | solution.py:59
  62.7 9.1 %collective-permute-start.6 = (f32[264,128]{1,0:T(8,128)S(1)}, f32[264,128]{1,0:T(8,128)S(1)}, u32[]{:S(2)}, u32[]{:S(2)}) collective-permute-start(f32[264,128]{1,0:T(8,128)S(1)} %pad_maximum_fusion.3), channel_id=1, source_target_pairs={{0,32},{4,36},{8,40},{12,44},{16,48},{20,52},{24,56},{28,60},{32,0... | collective-permute-start | bytes 405512 | tf_op jit(solution)/shard_map/ppermute | solution.py:59
  71.8 10.3 %collective-permute-done.6 = f32[264,128]{1,0:T(8,128)S(1)} collective-permute-done((f32[264,128]{1,0:T(8,128)S(1)}, f32[264,128]{1,0:T(8,128)S(1)}, u32[]{:S(2)}, u32[]{:S(2)}) %collective-permute-start.6) | collective-permute-done | bytes 135200 | tf_op jit(solution)/shard_map/ppermute | solution.py:59
  82.8 13.4 %collective-permute-start.7 = (f32[264,128]{1,0:T(8,128)S(1)}, f32[264,128]{1,0:T(8,128)S(1)}, u32[]{:S(2)}, u32[]{:S(2)}) collective-permute-start(f32[264,128]{1,0:T(8,128)S(1)} %pad_maximum_fusion.4), channel_id=1, source_target_pairs={{0,64},{4,68},{8,72},{12,76},{16,80},{20,84},{24,88},{28,92},{32,9... | collective-permute-start | bytes 405512 | tf_op jit(solution)/shard_map/ppermute | solution.py:59
  96.4 12.3 %collective-permute-done.7 = f32[264,128]{1,0:T(8,128)S(1)} collective-permute-done((f32[264,128]{1,0:T(8,128)S(1)}, f32[264,128]{1,0:T(8,128)S(1)}, u32[]{:S(2)}, u32[]{:S(2)}) %collective-permute-start.7) | collective-permute-done | bytes 135200 | tf_op jit(solution)/shard_map/ppermute | solution.py:59
  109.5 3.7 %collective-permute-start.8 = (f32[264,128]{1,0:T(8,128)S(1)}, f32[264,128]{1,0:T(8,128)S(1)}, u32[]{:S(2)}, u32[]{:S(2)}) collective-permute-start(f32[264,128]{1,0:T(8,128)S(1)} %pad_maximum_fusion.5), channel_id=1, source_target_pairs={{0,128},{4,132},{8,136},{12,140},{16,144},{20,148},{24,152},{28,15... | collective-permute-start | bytes 405512 | tf_op jit(solution)/shard_map/ppermute | solution.py:59
  113.7 3.1 %collective-permute-done.8 = f32[264,128]{1,0:T(8,128)S(1)} collective-permute-done((f32[264,128]{1,0:T(8,128)S(1)}, f32[264,128]{1,0:T(8,128)S(1)}, u32[]{:S(2)}, u32[]{:S(2)}) %collective-permute-start.8) | collective-permute-done | bytes 135200 | tf_op jit(solution)/shard_map/ppermute | solution.py:59
  117.6 3.9 %collective-permute-start.9 = (f32[264,128]{1,0:T(8,128)S(1)}, f32[264,128]{1,0:T(8,128)S(1)}, u32[]{:S(2)}, u32[]{:S(2)}) collective-permute-start(f32[264,128]{1,0:T(8,128)S(1)} %pad_maximum_fusion.6), channel_id=1, source_target_pairs={{0,256},{4,260},{8,264},{12,268},{16,272},{20,276},{24,280},{28,28... | collective-permute-start | bytes 405512 | tf_op jit(solution)/shard_map/ppermute | solution.py:59
  121.9 4.1 %collective-permute-done.9 = f32[264,128]{1,0:T(8,128)S(1)} collective-permute-done((f32[264,128]{1,0:T(8,128)S(1)}, f32[264,128]{1,0:T(8,128)S(1)}, u32[]{:S(2)}, u32[]{:S(2)}) %collective-permute-start.9) | collective-permute-done | bytes 135200 | tf_op jit(solution)/shard_map/ppermute | solution.py:59
  131.0 55.8 %all-reduce.2.cloned.1.call-done = f32[64,4,1024]{2,0,1:T(8,128)} async-done(((f32[64,4,1024]{2,0,1:T(8,128)}), f32[64,4,1024]{2,0,1:T(8,128)}) %all-reduce.2.cloned.1.call-update) | async-done | bytes 1048592 | tf_op jit(solution)/shard_map/psum | solution.py:159
  186.8 1.5 fusion.63
  191.2 2.5 %fusion.9 = f32[64,4,1024]{2,0,1:T(8,128)} fusion(bf16[512,1024]{1,0:T(8,128)(2,1)S(1)} %copy-done, f32[64,4,512]{2,0,1:T(8,128)S(1)} %get-tuple-element.45, u8[64,512]{1,0:T(8,128)(4,1)S(1)} %get-tuple-element.6, u8[64,512]{1,0:T(8,128)(4,1)S(1)} %get-tuple-element.5), kind=kOutput, calls=%fused_computation.16 | convolution fusion | flops 277610496 | bytes 2686976 | tf_op jit(solution)/shard_map/rtf,fd->rtd/dot_general | solution.py:170
  193.7 32.6 %reduce-scatter.2.cloned.1.call-done = f32[16,4,1024]{2,0,1:T(8,128)} async-done(((f32[64,4,1024]{2,0,1:T(8,128)}), f32[16,4,1024]{2,0,1:T(8,128)}) %reduce-scatter.2.cloned.1.call-update) | async-done | bytes 262160 | tf_op jit(solution)/shard_map/reduce_scatter | solution.py:169
  (194 shorter events, 27.7 us)
Async XLA Ops:
  6.5 184.6 %copy-start = (bf16[512,1024]{1,0:T(8,128)(2,1)S(1)}, bf16[512,1024]{1,0:T(8,128)(2,1)}, u32[]{:S(2)}) copy-start(bf16[512,1024]{1,0:T(8,128)(2,1)} %param.34) | copy-start | bytes 3145732
  6.5 180.3 %all-reduce.2.cloned.1.call-start = ((), (), s32[]{:S(2)}) async-start(), calls=%async_computation.1 | async-start | bytes 2097152 | tf_op jit(solution)/shard_map/psum | solution.py:159
  7.6 12.9 %collective-permute-start = (bf16[16,4,1024]{2,0,1:T(8,128)(2,1)S(1)}, bf16[16,4,1024]{2,0,1:T(8,128)(2,1)S(1)}, u32[]{:S(2)}, u32[]{:S(2)}) collective-permute-start(bf16[16,4,1024]{2,0,1:T(8,128)(2,1)S(1)} %copy.131), channel_id=1, source_target_pairs={{0,1},{1,2},{2,3},{3,0},{4,5},{5,6},{6,7},{7,4},{8,9},{9,10},{10,1... | collective-permute-start | bytes 393224 | tf_op jit(solution)/shard_map/ppermute | solution.py:107
  11.0 18.5 %collective-permute-start.2 = (bf16[16,4,1024]{2,0,1:T(8,128)(2,1)S(1)}, bf16[16,4,1024]{2,0,1:T(8,128)(2,1)S(1)}, u32[]{:S(2)}, u32[]{:S(2)}) collective-permute-start(bf16[16,4,1024]{2,0,1:T(8,128)(2,1)S(1)} %copy.131), channel_id=1, source_target_pairs={{0,3},{1,0},{2,1},{3,2},{4,7},{5,4},{6,5},{7,6},{8,11},{9,8},{10,9... | collective-permute-start | bytes 393224 | tf_op jit(solution)/shard_map/ppermute | solution.py:110
  16.1 1.5 copy-start.21
  18.6 1.4 copy-start.5
  20.4 2.2 copy-start.19
  20.5 8.1 %collective-permute-start.1 = (bf16[16,4,1024]{2,0,1:T(8,128)(2,1)S(1)}, bf16[16,4,1024]{2,0,1:T(8,128)(2,1)S(1)}, u32[]{:S(2)}, u32[]{:S(2)}) collective-permute-start(bf16[16,4,1024]{2,0,1:T(8,128)(2,1)S(1)} %collective-permute-done), channel_id=1, source_target_pairs={{0,1},{1,2},{2,3},{3,0},{4,5},{5,6},{6,7},{7,4},{8,9},{9,10},{10,1... | collective-permute-start | bytes 393224 | tf_op jit(solution)/shard_map/ppermute | solution.py:107
  31.9 2.7 %copy-start.9 = (bf16[64,4,2,64]{3,2,0,1:T(2,128)(2,1)}, bf16[64,4,2,64]{3,2,0,1:T(2,128)(2,1)S(1)}, u32[]{:S(2)}) copy-start(bf16[64,4,2,64]{3,2,0,1:T(2,128)(2,1)S(1)} %reshape.249) | copy-start | bytes 196612
  35.1 1.4 copy-start.6
  38.1 3.2 %collective-permute-start.3 = (f32[264,128]{1,0:T(8,128)S(1)}, f32[264,128]{1,0:T(8,128)S(1)}, u32[]{:S(2)}, u32[]{:S(2)}) collective-permute-start(f32[264,128]{1,0:T(8,128)S(1)} %pad_maximum_fusion), channel_id=1, source_target_pairs={{0,4},{4,0},{8,12},{12,8},{16,20},{20,16},{24,28},{28,24},{32,36},... | collective-permute-start | bytes 405512 | tf_op jit(solution)/shard_map/ppermute | solution.py:59
  42.1 7.7 %collective-permute-start.4 = (f32[264,128]{1,0:T(8,128)S(1)}, f32[264,128]{1,0:T(8,128)S(1)}, u32[]{:S(2)}, u32[]{:S(2)}) collective-permute-start(f32[264,128]{1,0:T(8,128)S(1)} %pad_maximum_fusion.1), channel_id=1, source_target_pairs={{0,8},{4,12},{8,0},{12,4},{16,24},{20,28},{24,16},{28,20},{32,40},... | collective-permute-start | bytes 405512 | tf_op jit(solution)/shard_map/ppermute | solution.py:59
  50.6 11.3 %collective-permute-start.5 = (f32[264,128]{1,0:T(8,128)S(1)}, f32[264,128]{1,0:T(8,128)S(1)}, u32[]{:S(2)}, u32[]{:S(2)}) collective-permute-start(f32[264,128]{1,0:T(8,128)S(1)} %pad_maximum_fusion.2), channel_id=1, source_target_pairs={{0,16},{4,20},{8,24},{12,28},{16,0},{20,4},{24,8},{28,12},{32,48},... | collective-permute-start | bytes 405512 | tf_op jit(solution)/shard_map/ppermute | solution.py:59
  62.7 19.4 %collective-permute-start.6 = (f32[264,128]{1,0:T(8,128)S(1)}, f32[264,128]{1,0:T(8,128)S(1)}, u32[]{:S(2)}, u32[]{:S(2)}) collective-permute-start(f32[264,128]{1,0:T(8,128)S(1)} %pad_maximum_fusion.3), channel_id=1, source_target_pairs={{0,32},{4,36},{8,40},{12,44},{16,48},{20,52},{24,56},{28,60},{32,0... | collective-permute-start | bytes 405512 | tf_op jit(solution)/shard_map/ppermute | solution.py:59
  82.8 13.5 %copy-start.7 = (bf16[64,4,128]{2,0,1:T(8,128)(2,1)S(1)}, bf16[64,4,128]{2,0,1:T(8,128)(2,1)}, u32[]{:S(2)}) copy-start(bf16[64,4,128]{2,0,1:T(8,128)(2,1)} %get-tuple-element.41) | copy-start | bytes 196612
  82.8 25.9 %collective-permute-start.7 = (f32[264,128]{1,0:T(8,128)S(1)}, f32[264,128]{1,0:T(8,128)S(1)}, u32[]{:S(2)}, u32[]{:S(2)}) collective-permute-start(f32[264,128]{1,0:T(8,128)S(1)} %pad_maximum_fusion.4), channel_id=1, source_target_pairs={{0,64},{4,68},{8,72},{12,76},{16,80},{20,84},{24,88},{28,92},{32,9... | collective-permute-start | bytes 405512 | tf_op jit(solution)/shard_map/ppermute | solution.py:59
  109.4 3.7 %copy-start.10 = (bf16[64,4,2,64]{3,2,0,1:T(2,128)(2,1)S(1)}, bf16[64,4,2,64]{3,2,0,1:T(2,128)(2,1)}, u32[]{:S(2)}) copy-start(bf16[64,4,2,64]{3,2,0,1:T(2,128)(2,1)} %copy-done.9) | copy-start | bytes 196612
  109.5 7.4 %collective-permute-start.8 = (f32[264,128]{1,0:T(8,128)S(1)}, f32[264,128]{1,0:T(8,128)S(1)}, u32[]{:S(2)}, u32[]{:S(2)}) collective-permute-start(f32[264,128]{1,0:T(8,128)S(1)} %pad_maximum_fusion.5), channel_id=1, source_target_pairs={{0,128},{4,132},{8,136},{12,140},{16,144},{20,148},{24,152},{28,15... | collective-permute-start | bytes 405512 | tf_op jit(solution)/shard_map/ppermute | solution.py:59
  117.6 8.4 %collective-permute-start.9 = (f32[264,128]{1,0:T(8,128)S(1)}, f32[264,128]{1,0:T(8,128)S(1)}, u32[]{:S(2)}, u32[]{:S(2)}) collective-permute-start(f32[264,128]{1,0:T(8,128)S(1)} %pad_maximum_fusion.6), channel_id=1, source_target_pairs={{0,256},{4,260},{8,264},{12,268},{16,272},{20,276},{24,280},{28,28... | collective-permute-start | bytes 405512 | tf_op jit(solution)/shard_map/ppermute | solution.py:59
  130.7 56.1 %copy-start.11 = (f32[1024]{0:T(1024)S(1)}, f32[1024]{0:T(1024)}, u32[]{:S(2)}) copy-start(f32[1024]{0:T(1024)} %param.29) | copy-start | bytes 12292
  130.7 95.5 %reduce-scatter.2.cloned.1.call-start = ((), (), s32[]{:S(2)}) async-start(), calls=%async_computation.2 | async-start | bytes 1310720 | tf_op jit(solution)/shard_map/reduce_scatter | solution.py:169
  186.8 1.5 copy-start.1
  193.7 32.6 %copy-start.12 = (f32[1024]{0:T(1024)S(1)}, f32[1024]{0:T(1024)}, u32[]{:S(2)}) copy-start(f32[1024]{0:T(1024)} %param.35) | copy-start | bytes 12292
  226.3 1.4 copy-start.16
  (12 other events, 11.0 us)
Sparse Core Ops, SparseCore 0:
  130.9 55.8 all-reduce.1
  193.8 32.4 reduce-scatter.1
